TPU v7x, 512 devices: a whole 4x8x8 slice. The times are simulated.
512 devices in a mesh: row: 16 (over z, core), col: 32 (over y, x).
Axes of the slice: x: 4, y: 8, z: 8, core: 2. Of those that a mesh axis runs over, the one named last changes fastest.
Arguments:
- a11: float32 [256, 256], replicated, may hold values from -1 to 400, as said below
- l11_bar: float32 [256, 256], replicated, may hold values from -24 to 24
- a21: float32 [32768, 256], P(('col', 'row')), may hold values from -72 to 72
- l21_bar: float32 [32768, 256], P(('col', 'row')), may hold values from -6 to 6
- s_bar: bfloat16 [32, 16, 64, 32768], P(None, 'row', None, 'col'), may hold values from -0.0625 to 0.0625
Outputs:
- a21_bar: float32 [32768, 256], P(('col', 'row'))
- a11_bar: float32 [256, 256], replicated
Inputs may be any that keep to these rules, and one draw needn't show every extreme that they name: a11 is symmetric and each diagonal entry exceeds the sum of the magnitudes of the other entries of its row.
All inputs are finite; a program needn't handle non-finite values.
Results may differ from a plain program's by a relative error of at most 0.0036.
Values may be sent and summed in bfloat16 or wider, within the bound.
No kernel may reach another device: no remote copies, remote signals or barrier semaphores. Data moves between devices by JAX's collectives and lax.ppermute only.
A program may use at most 64 MiB of HBM per device.

v0:
```python
import jax
import jax.numpy as jnp
from jax import lax
from jax.sharding import PartitionSpec as P


def halve_lower(square):
    lower = jnp.tril(square)
    return lower - 0.5 * jnp.diag(jnp.diag(square))


def right_solve_t(factor, rhs):
    return lax.linalg.triangular_solve(factor, rhs, left_side=False, lower=True, transpose_a=True)


def right_solve(factor, rhs):
    return lax.linalg.triangular_solve(factor, rhs, left_side=False, lower=True, transpose_a=False)


def left_solve_t(factor, rhs):
    return lax.linalg.triangular_solve(factor, rhs, left_side=True, lower=True, transpose_a=True)


def inner_rows(left, right):
    return lax.dot_general(
        left, right, (((0,), (0,)), ((), ())), preferred_element_type=jnp.float32
    )


def body(a11, l11_bar, a21, l21_bar, s_bar):
    highest = lax.Precision.HIGHEST
    rows_own = a21.shape[0]
    blocks_here = s_bar.shape[0]
    tile = s_bar.reshape(blocks_here * rows_own, s_bar.shape[3])
    l11 = jnp.linalg.cholesky(a11)
    l21_own = right_solve_t(l11, a21)
    panel_own = l21_own.astype(jnp.bfloat16)
    panel_rows = lax.all_gather(panel_own, "col", axis=0, tiled=True)
    panel_cols = lax.all_gather(panel_own, "row", axis=0, tiled=True)
    strip = tile
    row_share = lax.psum_scatter(
        jnp.dot(strip, panel_cols, preferred_element_type=jnp.float32),
        "col",
        scatter_dimension=0,
        tiled=True,
    )
    strip = tile
    col_share = lax.psum_scatter(
        inner_rows(strip, panel_rows), "row", scatter_dimension=0, tiled=True
    )
    trail = l21_bar - row_share - col_share
    a21_bar = right_solve(l11, trail)
    panel_exact = panel_own.astype(jnp.float32)
    coupling = lax.psum(jnp.dot(trail.T, panel_exact, precision=highest), ("row", "col"))
    l11_total = l11_bar - left_solve_t(l11, coupling)
    middle = halve_lower(jnp.dot(l11.T, l11_total, precision=highest))
    left = left_solve_t(l11, middle)
    whole = right_solve(l11, left)
    a11_bar = 0.5 * (whole + whole.T)
    return (a21_bar, a11_bar)


def solution(mesh):
    in_specs = (
        P(),
        P(),
        P(("col", "row"), None),
        P(("col", "row"), None),
        P(None, "row", None, "col"),
    )
    out_specs = (P(("col", "row"), None), P())
    return jax.shard_map(body, mesh=mesh, in_specs=in_specs, out_specs=out_specs, check_vma=False)
```

profile of v0, /device:TPU:23, one launch (start us, length us, event | category | flops | bytes accessed | tf_op | source)
XLA Modules:
  0.0 740.2 jit_solution(10154742874111276805)
XLA Ops:
  7.2 1.1 copy.13
  8.3 1.0 fusion.4
  9.3 11.7 %cholesky.50 = f32[128,128]{1,0:T(8,128)S(1)} custom-call(f32[128,128]{1,0:T(8,128)S(1)} %cholesky.118), custom_call_target="Cholesky" | custom-call | tf_op jit(solution)/shard_map/jit(cholesky)/cholesky | solution.py:35
  21.1 9.8 %custom-call.21 = f32[1,128,128]{1,2,0:T(8,128)S(1)} custom-call(f32[1,128,128]{2,1,0:T(8,128)S(1)} %get-tuple-element.40), custom_call_target="InvertDiagBlocksLowerTriangular" | custom-call | tf_op jit(solution)/shard_map/jit(cholesky)/cholesky | solution.py:35
  30.9 0.2 constant_dynamic-update-slice_fusion.1
  31.1 0.3 convolution_subtract_fusion.3
  31.4 11.7 %cholesky.105 = f32[128,128]{1,0:T(8,128)S(1)} custom-call(f32[128,128]{1,0:T(8,128)S(1)} %convolution_subtract_fusion.3), custom_call_target="Cholesky" | custom-call | tf_op jit(solution)/shard_map/jit(cholesky)/cholesky | solution.py:35
  43.1 0.6 compare_reduce_fusion
  45.0 0.1 triangular_solve.101
  45.1 4.0 while.5
  45.3 0.6 fusion.56
  45.8 1.3 bitcast_dynamic-update-slice_fusion.2
  47.2 0.6 fusion.56
  47.8 1.3 bitcast_dynamic-update-slice_fusion.2
  49.1 19.7 %custom-call.22 = f32[2,128,128]{1,2,0:T(8,128)S(1)} custom-call(f32[2,128,128]{2,1,0:T(8,128)S(1)} %get-tuple-element.18), custom_call_target="InvertDiagBlocksLowerTriangular" | custom-call | tf_op jit(solution)/shard_map/triangular_solve | solution.py:13
  68.7 0.9 fusion.23
  69.7 1.0 convolution_subtract_fusion.5
  70.7 0.2 convolution_convert_fusion
  70.9 0.6 pad_maximum_fusion.4
  71.6 79.2 %all-gather.2.cloned.1.call-done = bf16[2048,256]{1,0:T(8,128)(2,1)} async-done(((bf16[64,256]{1,0:T(8,128)(2,1)}), bf16[2048,256]{1,0:T(8,128)(2,1)}) %all-gather.2.cloned.1.call-update) | async-done | bytes 1048592 | tf_op jit(solution)/shard_map/all_gather | solution.py:38
  150.8 3.8 convolution_bitcast_fusion.1
  154.6 1.3 copy.19
  156.0 25.2 %all_gather.6 = bf16[1024,256]{1,0:T(8,128)(2,1)S(1)} all-gather(bf16[64,256]{1,0:T(8,128)(2,1)S(1)} %copy-done), channel_id=1, replica_groups=mesh['row'=16,'col'=32] {'row'}, dimensions={0}, use_global_device_ids=true | all-gather | bytes 557056 | tf_op jit(solution)/shard_map/all_gather | solution.py:39
  181.2 3.5 convolution_bitcast_fusion
  184.8 1.9 copy.17
  186.7 33.0 %reduce-scatter.9.cloned.1.call-done = f32[64,256]{1,0:T(8,128)} async-done(((f32[1024,256]{1,0:T(8,128)}), f32[64,256]{1,0:T(8,128)}) %reduce-scatter.9.cloned.1.call-update) | async-done | bytes 65552 | tf_op jit(solution)/shard_map/reduce_scatter | solution.py:48
  219.7 222.1 %reduce-scatter.7.cloned.1.call-done = f32[64,256]{1,0:T(8,128)} async-done(((f32[2048,256]{1,0:T(8,128)}), f32[64,256]{1,0:T(8,128)}) %reduce-scatter.7.cloned.1.call-update) | async-done | bytes 65552 | tf_op jit(solution)/shard_map/reduce_scatter | solution.py:41
  441.8 0.9 subtract_subtract_fusion
  442.7 1.0 fusion.36
  443.7 0.2 fusion.24
  444.0 0.2 convolution_subtract_fusion.4
  444.2 0.2 fusion.22
  444.4 0.6 pad_maximum_fusion.3
  445.1 280.3 %all-reduce.3.cloned.1.call-done = f32[256,256]{1,0:T(8,128)} async-done(((f32[256,256]{1,0:T(8,128)}), f32[256,256]{1,0:T(8,128)}) %all-reduce.3.cloned.1.call-update) | async-done | bytes 262160 | tf_op jit(solution)/shard_map/psum | solution.py:54
  725.3 1.2 fusion.11
  726.5 1.2 convolution_subtract_fusion.2
  727.7 0.3 fusion.19
  728.0 0.5 fusion
  728.5 2.3 gather_fusion
  730.9 0.1 multiply_subtract_fusion
  731.0 0.3 fusion.9
  731.2 0.3 convolution_subtract_fusion.1
  731.6 0.3 fusion.20
  731.8 0.3 fusion.7
  732.1 0.4 convolution_subtract_fusion
  732.5 0.3 fusion.21
  732.8 0.1 copy.16
  733.0 0.7 fusion.3
  (26 shorter events, 0.4 us)
Async XLA Ops:
  7.2 143.7 %all-gather.2.cloned.1.call-start = ((), (), s32[]{:S(2)}) async-start(), calls=%async_computation.2 | async-start | bytes 1081344 | tf_op jit(solution)/shard_map/all_gather | solution.py:38
  71.6 148.2 %reduce-scatter.9.cloned.1.call-start = ((), (), s32[]{:S(2)}) async-start(), calls=%async_computation.5 | async-start | bytes 1114112 | tf_op jit(solution)/shard_map/reduce_scatter | solution.py:48
  150.8 5.2 copy-start
  156.0 285.8 %reduce-scatter.7.cloned.1.call-start = ((), (), s32[]{:S(2)}) async-start(), calls=%async_computation.4 | async-start | bytes 2162688 | tf_op jit(solution)/shard_map/reduce_scatter | solution.py:41
  184.8 257.1 %copy-start.2 = (f32[64,256]{1,0:T(8,128)S(1)}, f32[64,256]{1,0:T(8,128)}, u32[]{:S(2)}) copy-start(f32[64,256]{1,0:T(8,128)} %param.10) | copy-start | bytes 196612
  184.8 543.2 %copy-start.1 = (f32[256,256]{1,0:T(8,128)S(1)}, f32[256,256]{1,0:T(8,128)}, u32[]{:S(2)}) copy-start(f32[256,256]{1,0:T(8,128)} %param.8) | copy-start | bytes 786436
  186.7 538.6 %all-reduce.3.cloned.1.call-start = ((), (), s32[]{:S(2)}) async-start(), calls=%async_computation.3 | async-start | bytes 524288 | tf_op jit(solution)/shard_map/psum | solution.py:54
Sparse Core Ops, SparseCore 0:
  71.7 79.0 all-gather.1
  156.1 63.5 reduce-scatter.8
  224.1 217.6 reduce-scatter.6
  447.2 278.0 all-reduce.2
where the time goes:
time: 741 us; the launch traced here: 740 us
  waiting for transfers between devices  615 us (83%)
  other arithmetic  57.7 us (8%)
  blocking collectives  25.2 us (3%)
  matrix products  16.5 us (2%)
  between operations  15.3 us (2%)
  local copies, waits for them, and re-layouts  10.7 us (1%)
    psum x1, waiting for transfers between devices, body(): lax.psum(jnp.dot(trail.T, panel_exact, precision=highest), ('row', 'col'))  280 us
    reduce_scatter x1, waiting for transfers between devices, body(): lax.psum_scatter(jnp.dot(strip, panel_cols, preferred_element_type=jnp.fl...  222 us
    all_gather x1, waiting for transfers between devices, body(): panel_rows = lax.all_gather(panel_own, 'col', axis=0, tiled=True)  79.2 us
    another operation x6, other arithmetic, body(): l11 = jnp.linalg.cholesky(a11)  33.9 us
    reduce_scatter x1, waiting for transfers between devices, body(): lax.psum_scatter(inner_rows(strip, panel_rows), 'row', scatter_dimension=...  33 us
    all_gather x1, blocking collectives, body(): panel_cols = lax.all_gather(panel_own, 'row', axis=0, tiled=True)  25.2 us
    another operation x5, other arithmetic, right_solve_t(): lax.linalg.triangular_solve(factor, rhs, left_side=False, lower=True, tra...  20.3 us
  transfers between devices with their start and end apart: 4, of which 4 were waited for; matrix products, arithmetic and copies ran while one was open for 1% of the time, Pallas kernels for 0%

commit v1 on v0

--- a/solution.py
+++ b/solution.py
@@ -1,7 +1,17 @@
+import functools
 import jax
 import jax.numpy as jnp
 from jax import lax
 from jax.sharding import PartitionSpec as P
+
+
+def wait_block(tile_in, mesh_ax):
+    return jnp.concatenate(
+        lax.all_to_all(jnp.stack(lax.axis_size(mesh_ax) * [tile_in], axis=0), mesh_ax, 0, 0), axis=0
+    )
+
+
+circles_apply = functools.partial(wait_block, mesh_ax="col")
 
 
 def halve_lower(square):
@@ -35,7 +45,7 @@
     l11 = jnp.linalg.cholesky(a11)
     l21_own = right_solve_t(l11, a21)
     panel_own = l21_own.astype(jnp.bfloat16)
-    panel_rows = lax.all_gather(panel_own, "col", axis=0, tiled=True)
+    panel_rows = circles_apply(panel_own)
     panel_cols = lax.all_gather(panel_own, "row", axis=0, tiled=True)
     strip = tile
     row_share = lax.psum_scatter(

time: 741 us -> 694 us (0.937)
  waiting for transfers between devices: 615 us -> 533 us
  blocking collectives: 25.2 us -> 60.5 us
    all_gather x1 -> x0, waiting for transfers between devices: 79.2 us -> none  [body(): panel_rows = lax.all_gather(panel_own, 'col', axis=0, tiled=True)]
    all_to_all x0 -> x1, blocking collectives: none -> 34.2 us  [wait_block(): lax.all_to_all(jnp.stack(lax.axis_size(mesh_ax) * [tile_in], axis=0), mes...]
  transfers between devices with their start and end apart: 4 -> 3, of which waited for: 4 -> 3; matrix products, arithmetic and copies ran while one was open for 1% -> 1% of each run, Pallas kernels for 0% -> 0%
where the time goes in v1:
time: 694 us
  waiting for transfers between devices  533 us (77%)
  blocking collectives  60.5 us (9%)
  other arithmetic  57.1 us (8%)
  matrix products  16.2 us (2%)
  between operations  15.4 us (2%)
  local copies, waits for them, and re-layouts  11 us (2%)
    psum x1, waiting for transfers between devices, body(): lax.psum(jnp.dot(trail.T, panel_exact, precision=highest), ('row', 'col'))  280 us
    reduce_scatter x1, waiting for transfers between devices, body(): lax.psum_scatter(jnp.dot(strip, panel_cols, preferred_element_type=jnp.fl...  222 us
    all_to_all x1, blocking collectives, wait_block(): lax.all_to_all(jnp.stack(lax.axis_size(mesh_ax) * [tile_in], axis=0), mes...  34.2 us
    another operation x6, other arithmetic, body(): l11 = jnp.linalg.cholesky(a11)  34 us
    reduce_scatter x1, waiting for transfers between devices, body(): lax.psum_scatter(inner_rows(strip, panel_rows), 'row', scatter_dimension=...  30.7 us
    all_gather x1, blocking collectives, body(): panel_cols = lax.all_gather(panel_own, 'row', axis=0, tiled=True)  26.3 us
    another operation x5, other arithmetic, right_solve_t(): lax.linalg.triangular_solve(factor, rhs, left_side=False, lower=True, tra...  19.7 us
  transfers between devices with their start and end apart: 3, of which 3 were waited for; matrix products, arithmetic and copies ran while one was open for 1% of the time, Pallas kernels for 0%

profile of v1, /device:TPU:23, one launch (start us, length us, event | category | flops | bytes accessed | tf_op | source)
XLA Modules:
  0.0 693.5 jit_solution(13484699020758459778)
XLA Ops:
  7.2 1.1 copy.13
  8.3 1.0 fusion.4
  9.3 11.7 %cholesky.50 = f32[128,128]{1,0:T(8,128)S(1)} custom-call(f32[128,128]{1,0:T(8,128)S(1)} %cholesky.118), custom_call_target="Cholesky" | custom-call | tf_op jit(solution)/shard_map/jit(cholesky)/cholesky | solution.py:45
  21.1 9.8 %custom-call.21 = f32[1,128,128]{1,2,0:T(8,128)S(1)} custom-call(f32[1,128,128]{2,1,0:T(8,128)S(1)} %get-tuple-element.40), custom_call_target="InvertDiagBlocksLowerTriangular" | custom-call | tf_op jit(solution)/shard_map/jit(cholesky)/cholesky | solution.py:45
  30.9 0.2 constant_dynamic-update-slice_fusion.1
  31.1 0.3 convolution_subtract_fusion.3
  31.4 11.7 %cholesky.105 = f32[128,128]{1,0:T(8,128)S(1)} custom-call(f32[128,128]{1,0:T(8,128)S(1)} %convolution_subtract_fusion.3), custom_call_target="Cholesky" | custom-call | tf_op jit(solution)/shard_map/jit(cholesky)/cholesky | solution.py:45
  43.1 0.7 compare_reduce_fusion
  45.3 0.1 triangular_solve.101
  45.3 4.2 while.5
  45.5 0.6 fusion.56
  46.1 1.4 bitcast_dynamic-update-slice_fusion.2
  47.5 0.6 fusion.56
  48.1 1.4 bitcast_dynamic-update-slice_fusion.2
  49.6 19.7 %custom-call.22 = f32[2,128,128]{1,2,0:T(8,128)S(1)} custom-call(f32[2,128,128]{2,1,0:T(8,128)S(1)} %get-tuple-element.18), custom_call_target="InvertDiagBlocksLowerTriangular" | custom-call | tf_op jit(solution)/shard_map/triangular_solve | solution.py:23
  69.2 0.9 fusion.23
  70.2 1.0 convolution_subtract_fusion.5
  71.2 0.2 convolution_convert_fusion
  71.4 0.1 stack.2
  71.5 34.2 %all_to_all.5 = bf16[32,64,256]{2,1,0:T(8,128)(2,1)S(1)} all-to-all(bf16[32,64,256]{2,1,0:T(8,128)(2,1)S(1)} %stack.2), channel_id=1, replica_groups=mesh['row'=16,'col'=32] {'col'}, dimensions={0} | all-to-all | bytes 2097152 | tf_op jit(solution)/shard_map/all_to_all | solution.py:10
  105.7 3.5 convolution_bitcast_fusion.1
  109.2 1.3 copy.19
  110.6 26.3 %all_gather.3 = bf16[1024,256]{1,0:T(8,128)(2,1)S(1)} all-gather(bf16[64,256]{1,0:T(8,128)(2,1)S(1)} %pad_maximum_fusion.4), channel_id=1, replica_groups=mesh['row'=16,'col'=32] {'row'}, dimensions={0}, use_global_device_ids=true | all-gather | bytes 557056 | tf_op jit(solution)/shard_map/all_gather | solution.py:49
  136.9 3.5 convolution_bitcast_fusion
  140.5 1.9 copy.17
  142.4 30.7 %reduce-scatter.9.cloned.1.call-done = f32[64,256]{1,0:T(8,128)} async-done(((f32[1024,256]{1,0:T(8,128)}), f32[64,256]{1,0:T(8,128)}) %reduce-scatter.9.cloned.1.call-update) | async-done | bytes 65552 | tf_op jit(solution)/shard_map/reduce_scatter | solution.py:58
  173.1 221.8 %reduce-scatter.7.cloned.1.call-done = f32[64,256]{1,0:T(8,128)} async-done(((f32[2048,256]{1,0:T(8,128)}), f32[64,256]{1,0:T(8,128)}) %reduce-scatter.7.cloned.1.call-update) | async-done | bytes 65552 | tf_op jit(solution)/shard_map/reduce_scatter | solution.py:51
  394.9 0.9 subtract_subtract_fusion
  395.8 1.0 fusion.36
  396.9 0.2 fusion.24
  397.1 0.2 convolution_subtract_fusion.4
  397.3 0.2 fusion.22
  397.6 0.6 pad_maximum_fusion.3
  398.2 280.4 %all-reduce.3.cloned.1.call-done = f32[256,256]{1,0:T(8,128)} async-done(((f32[256,256]{1,0:T(8,128)}), f32[256,256]{1,0:T(8,128)}) %all-reduce.3.cloned.1.call-update) | async-done | bytes 262160 | tf_op jit(solution)/shard_map/psum | solution.py:64
  678.6 1.2 fusion.11
  679.8 1.2 convolution_subtract_fusion.2
  681.0 0.3 fusion.19
  681.3 0.5 fusion
  681.8 2.3 gather_fusion
  684.2 0.1 multiply_subtract_fusion
  684.3 0.3 fusion.9
  684.5 0.3 convolution_subtract_fusion.1
  684.8 0.3 fusion.20
  685.1 0.3 fusion.7
  685.4 0.4 convolution_subtract_fusion
  685.8 0.3 fusion.21
  686.1 0.1 copy.16
  686.2 0.7 fusion.3
  (23 shorter events, 0.4 us)
Async XLA Ops:
  7.2 166.0 %reduce-scatter.9.cloned.1.call-start = ((), (), s32[]{:S(2)}) async-start(), calls=%async_computation.5 | async-start | bytes 1114112 | tf_op jit(solution)/shard_map/reduce_scatter | solution.py:58
  110.5 284.4 %reduce-scatter.7.cloned.1.call-start = ((), (), s32[]{:S(2)}) async-start(), calls=%async_computation.4 | async-start | bytes 2162688 | tf_op jit(solution)/shard_map/reduce_scatter | solution.py:51
  140.4 254.5 %copy-start.1 = (f32[64,256]{1,0:T(8,128)S(1)}, f32[64,256]{1,0:T(8,128)}, u32[]{:S(2)}) copy-start(f32[64,256]{1,0:T(8,128)} %param.10) | copy-start | bytes 196612
  140.4 540.8 %copy-start = (f32[256,256]{1,0:T(8,128)S(1)}, f32[256,256]{1,0:T(8,128)}, u32[]{:S(2)}) copy-start(f32[256,256]{1,0:T(8,128)} %param.8) | copy-start | bytes 786436
  142.4 536.3 %all-reduce.3.cloned.1.call-start = ((), (), s32[]{:S(2)}) async-start(), calls=%async_computation.3 | async-start | bytes 524288 | tf_op jit(solution)/shard_map/psum | solution.py:64
Sparse Core Ops, SparseCore 0:
  110.6 62.4 reduce-scatter.8
  177.5 217.3 reduce-scatter.6
  400.5 278.0 all-reduce.2
